TPU v7x, 128 devices: a whole 4x4x4 slice. The times are simulated.
128 devices in a mesh: seq: 16 (over x_hi, z, core), tp: 8 (over y, x_lo).
Axes of the slice: x: 4 (x_hi: 2, x_lo: 2; x = x_hi * 2 + x_lo), y: 4, z: 4, core: 2. Of those that a mesh axis runs over, the one named last changes fastest.
Arguments:
- tokens: bfloat16 [4, 2048, 4096], P(None, 'seq', 'tp'), may hold values from -6 to 6
- new_tokens: bfloat16 [4, 4096], P(None, 'tp'), may hold values from -6 to 6
- w_qkv: bfloat16 [3, 4096, 4096], P(None, None, 'tp')
- w_out: bfloat16 [4096, 4096], P('tp')
- q_gain: float32 [4096], P('tp'), may hold values from 0.5 to 6
- k_gain: float32 [4096], P('tp'), may hold values from 0.5 to 6
- post_gain: float32 [4096], P('tp'), may hold values from 0.5 to 1.5
- lengths: int32 [4], replicated, may hold values from 1 to 2048, 6144 in all
Outputs:
- hidden_out: bfloat16 [4, 2048, 4096], P(None, 'seq', 'tp')
- new_out: bfloat16 [4, 4096], P(None, 'tp')
Inputs may be any that keep to these rules, and one draw needn't show every extreme that they name: `lengths`: one prompt has exactly 2048 live tokens.
All inputs are finite; a program needn't handle non-finite values.
Results may differ from a plain program's by a relative error of at most 0.012.
The roundings to bfloat16 on the way count: a program that leaves them out, or rounds other values in their place, can miss the bound.
Values may be sent and summed in bfloat16 or wider, within the bound.
No kernel may reach another device: no remote copies, remote signals or barrier semaphores. Data moves between devices by JAX's collectives and lax.ppermute only.
A program may use at most 128 MiB of HBM per device.

v0:
```python
from functools import partial

import jax
import jax.numpy as jnp
from jax import lax
from jax.sharding import PartitionSpec as P

HD = 128


rope_base = 500000.0
norm_eps = 1e-06
masked_fill = -1e30


def joined(value, axis, combine):
    everything = jax.tree.map(lambda part: lax.all_gather(part, axis), value)
    initial = jax.tree.map(lambda part: part[0], everything)

    def hop(k, so_far):
        return combine(so_far, jax.tree.map(lambda part: part[k], everything))

    return lax.fori_loop(1, lax.axis_size(axis), hop, initial)


def rotate(values, position):
    half = values.shape[-1] // 2
    freq = rope_base ** (-(jnp.arange(half, dtype=jnp.float32) * 2.0) / values.shape[-1])
    angle = position.astype(jnp.float32)[..., None] * freq
    cosine = jnp.cos(angle)
    sine = jnp.sin(angle)
    lower = values[..., :half]
    upper = values[..., half:]
    return jnp.concatenate([lower * cosine - upper * sine, upper * cosine + lower * sine], -1)


def fold_step(carry, pieces, start, queries, query_pos, lengths, scale):
    running_max, running_sum, running_acc = carry
    key_piece, value_piece = pieces
    count = key_piece.shape[1]
    scores = (
        jnp.einsum("sphe,snhe->shpn", queries, key_piece, preferred_element_type=jnp.float32)
        * scale
    )
    key_pos = jnp.arange(count, dtype=jnp.int32)
    valid = (key_pos[None, None, :] <= query_pos[None, :, None]) & (
        key_pos[None, None, :] < lengths[:, None, None]
    )
    valid = valid[:, None, :, :]
    scores = jnp.where(valid, scores, masked_fill)
    new_max = jnp.maximum(running_max, jnp.max(scores, -1))
    weights = jnp.where(valid, jnp.exp(scores - new_max[..., None]), 0.0)
    running_sum = jnp.sum(weights, -1)
    running_acc = jnp.einsum(
        "shpn,snhe->shpe",
        weights.astype(jnp.bfloat16),
        value_piece,
        preferred_element_type=jnp.float32,
    )
    return (new_max, running_sum, running_acc)


def combine(first, second):
    first_max, first_sum, first_acc = first
    second_max, second_sum, second_acc = second
    top = jnp.maximum(first_max, second_max)
    first_factor = jnp.exp(first_max - top)
    second_factor = jnp.exp(second_max - top)
    return (
        top,
        first_sum * first_factor + second_sum * second_factor,
        first_acc * first_factor[..., None] + second_acc * second_factor[..., None],
    )


def body(tokens, new_tokens, w_qkv, w_out, q_gain, k_gain, post_gain, lengths):
    seqs, pos_dev, width_local = tokens.shape
    heads_local = width_local // HD
    full_width = w_qkv.shape[1]
    prompt_rows = seqs * pos_dev
    flat_rows = tokens.reshape(prompt_rows, width_local)
    row_piece = lax.all_gather(flat_rows, "tp", axis=1, tiled=True)
    new_piece = lax.all_gather(new_tokens, "tp", axis=1, tiled=True)
    proj_rows = jnp.einsum("tn,cnf->ctf", row_piece, w_qkv, preferred_element_type=jnp.float32)
    proj_new = jnp.einsum("tn,cnf->ctf", new_piece, w_qkv, preferred_element_type=jnp.float32)
    query_rows, key_rows = (proj_rows[0], proj_rows[1])
    query_fresh, key_fresh = (proj_new[0], proj_new[1])
    query_sq, key_sq, query_new_sq, key_new_sq = lax.psum(
        (
            jnp.sum(query_rows * query_rows, -1),
            jnp.sum(key_rows * key_rows, -1),
            jnp.sum(query_fresh * query_fresh, -1),
            jnp.sum(key_fresh * key_fresh, -1),
        ),
        "tp",
    )

    def normed(values, square_sum, gain):
        return values * lax.rsqrt(square_sum[:, None] / full_width + norm_eps) * gain

    seq_index = lax.axis_index("seq")
    query_pos = seq_index * pos_dev + jnp.arange(pos_dev, dtype=jnp.int32)
    row_pos = jnp.tile(query_pos, seqs)
    queries = rotate(
        normed(query_rows, query_sq, q_gain).reshape(prompt_rows, heads_local, HD), row_pos[:, None]
    )
    queries = queries.astype(jnp.bfloat16).reshape(seqs, pos_dev, heads_local, HD)
    keys = rotate(
        normed(key_rows, key_sq, k_gain).reshape(prompt_rows, heads_local, HD), row_pos[:, None]
    )
    keys = keys.astype(jnp.bfloat16).reshape(seqs, pos_dev, heads_local, HD)
    values = proj_rows[2].astype(jnp.bfloat16).reshape(seqs, pos_dev, heads_local, HD)
    new_queries = rotate(
        normed(query_fresh, query_new_sq, q_gain).reshape(seqs, heads_local, HD), lengths[:, None]
    ).astype(jnp.bfloat16)
    new_keys = rotate(
        normed(key_fresh, key_new_sq, k_gain).reshape(seqs, heads_local, HD), lengths[:, None]
    ).astype(jnp.bfloat16)
    new_values = proj_new[2].astype(jnp.bfloat16).reshape(seqs, heads_local, HD)
    scale = HD ** (-0.5)
    start_carry = (
        jnp.full((seqs, heads_local, pos_dev), masked_fill, jnp.float32),
        jnp.zeros((seqs, heads_local, pos_dev), jnp.float32),
        jnp.zeros((seqs, heads_local, pos_dev, HD), jnp.float32),
    )
    stepper = partial(fold_step, queries=queries, query_pos=query_pos, lengths=lengths, scale=scale)
    final_max, final_sum, final_acc = stepper(
        start_carry,
        (
            lax.all_gather(keys, "seq", axis=1, tiled=True),
            lax.all_gather(values, "seq", axis=1, tiled=True),
        ),
        jnp.int32(0),
    )
    attention = (
        (final_acc / final_sum[..., None])
        .transpose(0, 2, 1, 3)
        .reshape(prompt_rows, width_local)
        .astype(jnp.bfloat16)
    )
    local_scores = (
        jnp.einsum("she,sphe->shp", new_queries, keys, preferred_element_type=jnp.float32) * scale
    )
    live = (query_pos[None, :] < lengths[:, None])[:, None, :]
    local_scores = jnp.where(live, local_scores, masked_fill)
    local_max = jnp.max(local_scores, -1)
    local_weights = jnp.where(live, jnp.exp(local_scores - local_max[..., None]), 0.0)
    local_sum = jnp.sum(local_weights, -1)
    local_acc = jnp.einsum(
        "shp,sphe->she",
        local_weights.astype(jnp.bfloat16),
        values,
        preferred_element_type=jnp.float32,
    )
    merged_max, merged_sum, merged_acc = joined((local_max, local_sum, local_acc), "seq", combine)
    self_score = (
        jnp.einsum("she,she->sh", new_queries, new_keys, preferred_element_type=jnp.float32) * scale
    )
    new_top = jnp.maximum(merged_max, self_score)
    keep_factor = jnp.exp(merged_max - new_top)
    own_weight = jnp.exp(self_score - new_top)
    new_total = merged_sum * keep_factor + own_weight
    own_rounded = lax.optimization_barrier(own_weight.astype(jnp.bfloat16)).astype(jnp.float32)
    numer = merged_acc * keep_factor[..., None] + own_rounded[..., None] * new_values.astype(
        jnp.float32
    )
    new_attention = (numer / new_total[..., None]).reshape(seqs, width_local).astype(jnp.bfloat16)
    part_rows = jnp.dot(attention, w_out, preferred_element_type=jnp.float32)
    part_new = jnp.dot(new_attention, w_out, preferred_element_type=jnp.float32)
    sum_rows, sum_new = (
        lax.psum(part_rows.astype(jnp.bfloat16), "tp").astype(jnp.float32),
        lax.psum(part_new.astype(jnp.bfloat16), "tp").astype(jnp.float32),
    )
    mean_rows = jnp.mean(sum_rows * sum_rows, -1)
    mean_new = jnp.mean(sum_new * sum_new, -1)
    offset = lax.axis_index("tp") * width_local
    own_rows = lax.dynamic_slice_in_dim(sum_rows, offset, width_local, 1)
    own_new = lax.dynamic_slice_in_dim(sum_new, offset, width_local, 1)
    out_rows = (
        flat_rows.astype(jnp.float32)
        + own_rows * lax.rsqrt(mean_rows[:, None] + norm_eps) * post_gain
    )
    out_new = (
        new_tokens.astype(jnp.float32)
        + own_new * lax.rsqrt(mean_new[:, None] + norm_eps) * post_gain
    )
    return (
        out_rows.astype(jnp.bfloat16).reshape(seqs, pos_dev, width_local),
        out_new.astype(jnp.bfloat16),
    )


def solution(mesh):
    in_specs = (
        P(None, "seq", "tp"),
        P(None, "tp"),
        P(None, None, "tp"),
        P("tp", None),
        P("tp"),
        P("tp"),
        P("tp"),
        P(),
    )
    out_specs = (P(None, "seq", "tp"), P(None, "tp"))
    return jax.shard_map(body, mesh=mesh, in_specs=in_specs, out_specs=out_specs, check_vma=False)
```

profile of v0, /device:TPU:32, one launch (start us, length us, event | category | flops | bytes accessed | tf_op | source)
XLA Modules:
  0.0 494.8 jit_solution(5832578119530907273)
XLA Ops:
  7.2 0.7 all-gather.9.cloned.1.call-update
  7.9 28.6 %all_gather.33 = bf16[4,4096]{1,0:T(4,128)(2,1)S(1)} all-gather(bf16[4,512]{1,0:T(4,128)(2,1)} %param.11), channel_id=1, replica_groups=mesh['seq'=16,'tp'=8] {'tp'}, dimensions={1}, use_global_device_ids=true | all-gather | bytes 36864 | tf_op jit(solution)/shard_map/all_gather | solution.py:83
  36.6 6.3 %convolution_bitcast_fusion = f32[3,4,512]{2,1,0:T(4,128)S(1)} fusion(bf16[3,4096,512]{2,1,0:T(8,128)(2,1)} %param.12, bf16[4,4096]{1,0:T(4,128)(2,1)S(1)} %all_gather.33), kind=kOutput, calls=%fused_computation.23 | convolution fusion | flops 50331648 | bytes 12640256 | tf_op jit(solution)/shard_map/tn,cnf->ctf/dot_general | solution.py:85
  42.9 0.2 multiply_reduce_fusion.4
  43.1 0.5 multiply_cosine_fusion
  43.6 59.1 %all-gather.9.cloned.1.call-done = bf16[512,4096]{1,0:T(8,128)(2,1)} async-done(((bf16[512,512]{1,0:T(8,128)(2,1)}), bf16[512,4096]{1,0:T(8,128)(2,1)}) %all-gather.9.cloned.1.call-update) | async-done | bytes 4194320 | tf_op jit(solution)/shard_map/all_gather | solution.py:82
  102.7 10.6 %fusion.11 = f32[3,512,512]{1,2,0:T(8,128)S(1)} fusion(bf16[3,4096,512]{2,1,0:T(8,128)(2,1)} %param.12, bf16[512,4096]{1,0:T(8,128)(2,1)} %all-gather.9.cloned.1.call-done), kind=kOutput, calls=%fused_computation.21 | convolution fusion | flops 6442450944 | bytes 19922944 | tf_op jit(solution)/shard_map/tn,cnf->ctf/dot_general | solution.py:84
  113.4 1.7 copy-done.1
  115.0 0.4 multiply_reduce_fusion.2
  115.4 18.1 %all-reduce = (f32[512]{0:T(512)S(1)}, f32[512]{0:T(512)S(1)}, f32[4]{0:T(128)S(1)}, f32[4]{0:T(128)S(1)}) all-reduce(f32[512]{0:T(512)S(1)} %get-tuple-element.184, f32[512]{0:T(512)S(1)} %get-tuple-element.183, f32[4]{0:T(128)S(1)} %get-tuple-element.186, f32[4]{0:T(128)S(1)} %get-tuple-element.185), channel_id=1, replica_groups=mesh['seq'=16,'tp'=8] {'tp'}, use_global_device_ids=true, to_apply=%region_3.0 | all-reduce | flops 1032 | bytes 8256 | tf_op jit(solution)/shard_map/psum | solution.py:88
  133.6 0.1 multiply_multiply_fusion
  133.7 0.1 multiply_multiply_fusion.1
  133.9 0.4 subtract_convert_fusion.1
  134.3 0.3 copy.22
  134.7 0.3 copy.23
  135.0 1.1 pad_maximum_fusion
  136.2 1.3 slice.118
  137.5 0.1 convert_element_type.91
  137.6 1.1 copy.24
  139.0 0.1 multiply_cosine_fusion.1
  139.2 0.2 iota_compare_fusion
  139.4 0.6 broadcast_and_fusion
  140.2 0.1 subtract_convert_fusion.2
  140.3 1.4 fusion.29
  141.7 0.1 fusion.32
  141.8 0.2 convert_bitcast_fusion
  142.0 1.3 fusion.27
  143.3 20.5 %all-gather.2 = f32[64,4,128]{2,1,0:T(4,128)S(1)} all-gather(f32[4,4,128]{2,1,0:T(4,128)S(1)} %bitcast.96), channel_id=4, replica_groups=mesh['seq'=16,'tp'=8] {'seq'}, dimensions={0}, use_global_device_ids=true | all-gather | bytes 139264 | tf_op jit(solution)/shard_map/all_gather | solution.py:17
  163.9 0.3 copy.20
  164.3 0.3 copy.21
  164.6 24.0 %all-gather.4 = f32[16,4,4]{2,1,0:T(4,128)S(1)} all-gather(f32[1,4,4]{2,1,0:T(4,128)S(1)} %bitcast.99), channel_id=3, replica_groups=mesh['seq'=16,'tp'=8] {'seq'}, dimensions={0}, use_global_device_ids=true | all-gather | bytes 1088 | tf_op jit(solution)/shard_map/all_gather | solution.py:17
  188.5 19.7 %all-gather.3 = f32[16,4,4]{2,1,0:T(4,128)S(1)} all-gather(f32[1,4,4]{2,1,0:T(4,128)S(1)} %bitcast.97), channel_id=2, replica_groups=mesh['seq'=16,'tp'=8] {'seq'}, dimensions={0}, use_global_device_ids=true | all-gather | bytes 1088 | tf_op jit(solution)/shard_map/all_gather | solution.py:17
  208.3 13.4 %fusion.3 = (f32[4,4,128]{2,1,0:T(4,128)S(1)}, f32[4,4,128,2048]{3,2,1,0:T(8,128)}) fusion(pred[4,128,2048]{2,1,0:T(8,128)(4,1)S(1)} %broadcast_and_fusion, bf16[4,2048,4,128]{3,1,2,0:T(8,128)(2,1)} %all-gather.11.cloned.1.call-done, bf16[4,128,4,64]{3,1,2,0:T(8,128)(2,1)S(1)} %copy.21, bf16[4,128,4,64]{3,1,2,0:T(8,128)(2,1)S(1)} %copy.20), kind=kOutput, calls=%fused_computation.10 | convolution fusion | flops 1087371264 | bytes 26746880 | tf_op jit(solution)/shard_map/sphe,snhe->shpn/dot_general | solution.py:42
  221.7 8.4 %fusion.4 = f32[4,4,128]{2,1,0:T(4,128)S(1)} fusion(f32[4,4,128,2048]{3,2,1,0:T(8,128)} %get-tuple-element.235, f32[4,4,128]{2,1,0:T(4,128)S(1)} %broadcast_maximum_fusion, pred[4,128,2048]{2,1,0:T(8,128)(4,1)S(1)} %broadcast_and_fusion), kind=kLoop, calls=%fused_computation.11 | loop fusion | flops 20969472 | bytes 17842176 | tf_op jit(solution)/shard_map/reduce_sum | solution.py:53
  230.1 51.2 %all-gather.13.cloned.1.call-done = bf16[4,2048,4,128]{3,1,2,0:T(8,128)(2,1)} async-done(((bf16[4,128,4,128]{3,1,2,0:T(8,128)(2,1)}), bf16[4,2048,4,128]{3,1,2,0:T(8,128)(2,1)}) %all-gather.13.cloned.1.call-update) | async-done | bytes 8388624 | tf_op jit(solution)/shard_map/all_gather | solution.py:131
  281.3 11.7 %divide_convert_fusion = bf16[4,128,4,128]{3,1,2,0:T(8,128)(2,1)S(1)} fusion(bf16[4,2048,4,128]{3,1,2,0:T(8,128)(2,1)} %all-gather.13.cloned.1.call-done, f32[4,4,128,2048]{3,2,1,0:T(8,128)} %get-tuple-element.235, f32[4,4,128]{2,1,0:T(4,128)S(1)} %broadcast_maximum_fusion, pred[4,128,2048]{2,1,0:T(8,128)(4,1)S(1)} %broadcast_and_fusion, ...), kind=kOutput, calls=%fused_computation.26 | convolution fusion | flops 1095237632 | bytes 26755072 | tf_op jit(solution)/shard_map/shpn,snhe->shpe/dot_general | solution.py:54
  293.0 0.4 copy.25
  293.4 4.3 convolution_convert_fusion
  297.8 1.6 while.19
  297.8 0.1 fusion.59
  297.9 0.1 fusion.59
  298.1 0.1 fusion.59
  298.2 0.1 fusion.59
  298.3 0.1 fusion.59
  298.4 0.1 fusion.59
  298.5 0.1 fusion.59
  298.6 0.1 fusion.59
  298.7 0.1 fusion.59
  298.8 0.1 fusion.59
  298.9 0.1 fusion.59
  299.0 0.1 fusion.59
  299.1 0.1 fusion.59
  299.2 0.1 fusion.59
  299.3 0.1 fusion.59
  299.4 0.2 fusion.26
  299.6 0.1 fusion.36
  299.7 2.8 convolution_convert_fusion.1
  302.5 35.0 %psum.47 = bf16[4,4096]{1,0:T(4,128)(2,1)S(1)} all-reduce(bf16[4,4096]{1,0:T(4,128)(2,1)S(1)} %convolution_convert_fusion.1), channel_id=1, replica_groups=mesh['seq'=16,'tp'=8] {'tp'}, use_global_device_ids=true, to_apply=%region_16.17 | all-reduce | flops 16384 | bytes 65536 | tf_op jit(solution)/shard_map/psum | solution.py:172
  337.6 0.1 multiply_reduce_fusion.3
  337.7 0.7 add_convert_fusion.3
  338.4 142.5 %all-reduce.3.cloned.1.call-done = bf16[512,4096]{1,0:T(8,128)(2,1)} async-done(((bf16[512,4096]{1,0:T(8,128)(2,1)}), bf16[512,4096]{1,0:T(8,128)(2,1)}) %all-reduce.3.cloned.1.call-update) | async-done | bytes 4194320 | tf_op jit(solution)/shard_map/psum | solution.py:171
  480.9 3.1 multiply_reduce_fusion
  484.0 3.3 convert_element_type.95
  487.3 1.0 add_convert_fusion
  (66 shorter events, 1.3 us)
Async XLA Ops:
  7.2 95.5 %all-gather.9.cloned.1.call-start = ((), (), s32[]{:S(2)}) async-start(), calls=%async_computation | async-start | bytes 4718592 | tf_op jit(solution)/shard_map/all_gather | solution.py:82
  7.9 200.4 %all-gather.11.cloned.1.call-start = ((), (), s32[]{:S(2)}) async-start(), calls=%async_computation.1 | async-start | bytes 8912896 | tf_op jit(solution)/shard_map/all_gather | solution.py:130
  43.6 89.9 %copy-start.5 = (f32[512]{0:T(512)S(1)}, f32[512]{0:T(512)}, u32[]{:S(2)}) copy-start(f32[512]{0:T(512)} %param.15) | copy-start | bytes 6148
  43.6 90.1 %copy-start.6 = (f32[512]{0:T(512)S(1)}, f32[512]{0:T(512)}, u32[]{:S(2)}) copy-start(f32[512]{0:T(512)} %param.14) | copy-start | bytes 6148
  113.3 1.7 copy-start.1
  115.4 23.4 %copy-start.7 = (s32[4]{0:T(128)S(1)}, s32[4]{0:T(128)}, u32[]{:S(2)}) copy-start(s32[4]{0:T(128)} %param.17) | copy-start | bytes 52
  136.2 145.1 %all-gather.13.cloned.1.call-start = ((), (), s32[]{:S(2)}) async-start(), calls=%async_computation.2 | async-start | bytes 8912896 | tf_op jit(solution)/shard_map/all_gather | solution.py:131
  138.8 342.1 %all-reduce.3.cloned.1.call-start = ((), (), s32[]{:S(2)}) async-start(), calls=%async_computation.3 | async-start | bytes 8388608 | tf_op jit(solution)/shard_map/psum | solution.py:171
  281.3 12.1 %copy-start = (bf16[512,4096]{1,0:T(8,128)(2,1)S(1)}, bf16[512,4096]{1,0:T(8,128)(2,1)}, u32[]{:S(2)}) copy-start(bf16[512,4096]{1,0:T(8,128)(2,1)} %param.13) | copy-start | bytes 12582916
  293.4 44.3 %copy-start.3 = (bf16[4,512]{1,0:T(4,128)(2,1)S(1)}, bf16[4,512]{1,0:T(4,128)(2,1)}, u32[]{:S(2)}) copy-start(bf16[4,512]{1,0:T(4,128)(2,1)} %param.11) | copy-start | bytes 12292
  293.4 44.3 %copy-start.4 = (f32[512]{0:T(512)S(1)}, f32[512]{0:T(512)}, u32[]{:S(2)}) copy-start(f32[512]{0:T(512)} %param.16) | copy-start | bytes 6148
  338.4 148.8 %copy-start.2 = (bf16[4,128,512]{2,1,0:T(8,128)(2,1)S(1)}, bf16[4,128,512]{2,1,0:T(8,128)(2,1)}, u32[]{:S(2)}) copy-start(bf16[4,128,512]{2,1,0:T(8,128)(2,1)} %param.10) | copy-start | bytes 1572868
Sparse Core Ops, SparseCore 0:
  9.6 93.0 all-gather.8
  136.3 70.8 all-gather.10
  210.2 71.0 all-gather.12
  297.9 182.9 all-reduce.2
where the time goes:
time: 496 us; the launch traced here: 495 us
  waiting for transfers between devices  254 us (51%)
  blocking collectives  146 us (29%)
  matrix products  51.9 us (10%)
  other arithmetic  23 us (5%)
  between operations  14.1 us (3%)
  local copies, waits for them, and re-layouts  6.25 us (1%)
    psum x1, waiting for transfers between devices, body(): lax.psum(part_rows.astype(jnp.bfloat16), 'tp').astype(jnp.float32)  142 us
    all_gather x3, blocking collectives, joined(): everything = jax.tree.map(lambda part: lax.all_gather(part, axis), value)  64.2 us
    all_gather x1, waiting for transfers between devices, body(): row_piece = lax.all_gather(flat_rows, 'tp', axis=1, tiled=True)  59.1 us
    all_gather x1, waiting for transfers between devices, body(): lax.all_gather(values, 'seq', axis=1, tiled=True)  51.2 us
    psum x1, blocking collectives, body(): lax.psum(part_new.astype(jnp.bfloat16), 'tp').astype(jnp.float32)  35 us
    all_gather x1, blocking collectives, body(): new_piece = lax.all_gather(new_tokens, 'tp', axis=1, tiled=True)  28.6 us
    psum x1, blocking collectives, body(): lax.psum((jnp.sum(query_rows * query_rows, -1), jnp.sum(key_rows * key_ro...  18.1 us
    dot_general x1, matrix products, fold_step(): jnp.einsum('sphe,snhe->shpn', queries, key_piece, preferred_element_type=...  13.4 us
  transfers between devices with their start and end apart: 4, of which 3 were waited for; matrix products, arithmetic and copies ran while one was open for 9% of the time, Pallas kernels for 0%

commit v1 on v0

v1 whole, which is shorter than its diff:
```python
import jax
import jax.numpy as jnp
from jax import lax
from jax.sharding import PartitionSpec as P

HD = 128


rope_base = 500000.0
norm_eps = 1e-06
masked_fill = -1e30


def rotate(values, position):
    half = values.shape[-1] // 2
    freq = rope_base ** (-(jnp.arange(half, dtype=jnp.float32) * 2.0) / values.shape[-1])
    angle = position.astype(jnp.float32)[..., None] * freq
    cosine = jnp.cos(angle)
    sine = jnp.sin(angle)
    lower = values[..., :half]
    upper = values[..., half:]
    return jnp.concatenate([lower * cosine - upper * sine, upper * cosine + lower * sine], -1)


def attend_pair(q_all, k_all, v_all, q_new, k_new, v_new, length):
    count = q_all.shape[0]
    scale = HD ** (-0.5)
    scores = jnp.dot(q_all, k_all.T, preferred_element_type=jnp.float32) * scale
    query_pos = jnp.arange(count, dtype=jnp.int32)[:, None]
    key_pos = jnp.arange(count, dtype=jnp.int32)[None, :]
    valid = (key_pos <= query_pos) & (key_pos < length)
    scores = jnp.where(valid, scores, masked_fill)
    top = jnp.max(scores, -1, keepdims=True)
    weights = jnp.where(valid, jnp.exp(scores - top), 0.0)
    total = jnp.sum(weights, -1, keepdims=True)
    prompt_out = (
        jnp.dot(weights.astype(jnp.bfloat16), v_all, preferred_element_type=jnp.float32) / total
    ).astype(jnp.bfloat16)
    new_scores = jnp.dot(k_all, q_new, preferred_element_type=jnp.float32) * scale
    live = jnp.arange(count, dtype=jnp.int32) < length
    new_scores = jnp.where(live, new_scores, masked_fill)
    self_score = jnp.dot(q_new, k_new, preferred_element_type=jnp.float32) * scale
    new_top = jnp.maximum(jnp.max(new_scores), self_score)
    new_weights = jnp.where(live, jnp.exp(new_scores - new_top), 0.0)
    own_weight = jnp.exp(self_score - new_top)
    new_total = jnp.sum(new_weights) + own_weight
    own_rounded = lax.optimization_barrier(own_weight.astype(jnp.bfloat16)).astype(jnp.float32)
    numer = jnp.dot(new_weights.astype(jnp.bfloat16), v_all, preferred_element_type=jnp.float32)
    numer = numer + own_rounded * v_new.astype(jnp.float32)
    return prompt_out, (numer / new_total).astype(jnp.bfloat16)


def body(tokens, new_tokens, w_qkv, w_out, q_gain, k_gain, post_gain, lengths):
    seqs, pos_dev, width_local = tokens.shape
    heads_local = width_local // HD
    full_width = w_qkv.shape[1]
    n_seq = lax.axis_size("seq")
    pairs = seqs * heads_local
    assert pairs == n_seq
    prompt_rows = seqs * pos_dev
    full_len = pos_dev * n_seq
    flat_rows = tokens.reshape(prompt_rows, width_local)
    local_rows = jnp.concatenate([flat_rows, new_tokens], 0)
    all_rows = lax.all_gather(local_rows, "tp", axis=1, tiled=True)
    proj = jnp.einsum("tn,cnf->ctf", all_rows, w_qkv, preferred_element_type=jnp.float32)
    query_raw, key_raw = proj[0], proj[1]
    query_sq, key_sq = lax.psum(
        (jnp.sum(query_raw * query_raw, -1), jnp.sum(key_raw * key_raw, -1)), "tp"
    )

    def normed(values, square_sum, gain):
        return values * lax.rsqrt(square_sum[:, None] / full_width + norm_eps) * gain

    seq_index = lax.axis_index("seq")
    query_pos = seq_index * pos_dev + jnp.arange(pos_dev, dtype=jnp.int32)
    row_pos = jnp.concatenate([jnp.tile(query_pos, seqs), lengths.astype(jnp.int32)], 0)
    rows_all = prompt_rows + seqs
    queries = rotate(
        normed(query_raw, query_sq, q_gain).reshape(rows_all, heads_local, HD), row_pos[:, None]
    ).astype(jnp.bfloat16)
    keys = rotate(
        normed(key_raw, key_sq, k_gain).reshape(rows_all, heads_local, HD), row_pos[:, None]
    ).astype(jnp.bfloat16)
    values = proj[2].astype(jnp.bfloat16).reshape(rows_all, heads_local, HD)

    qkv = jnp.stack([queries[:prompt_rows], keys[:prompt_rows], values[:prompt_rows]], 0)
    qkv = qkv.reshape(3, seqs, pos_dev, heads_local, HD).transpose(1, 3, 0, 2, 4)
    qkv = qkv.reshape(pairs, 3, pos_dev, HD)
    got = lax.all_to_all(qkv, "seq", 0, 0, tiled=True)
    full = got.transpose(1, 0, 2, 3).reshape(3, full_len, HD)

    owner = seq_index
    own_prompt = owner // heads_local
    new_q = queries[prompt_rows:].reshape(pairs, HD)[owner]
    new_k = keys[prompt_rows:].reshape(pairs, HD)[owner]
    new_v = values[prompt_rows:].reshape(pairs, HD)[owner]
    prompt_out, new_out = attend_pair(
        full[0], full[1], full[2], new_q, new_k, new_v, lengths[own_prompt]
    )

    pad = 8
    back = jnp.concatenate(
        [prompt_out.reshape(n_seq, pos_dev, HD), jnp.broadcast_to(new_out, (n_seq, pad, HD))], 1
    )
    ret = lax.all_to_all(back, "seq", 0, 0, tiled=True)
    ret = ret.reshape(seqs, heads_local, pos_dev + pad, HD)
    attn_rows = ret[:, :, :pos_dev].transpose(0, 2, 1, 3).reshape(prompt_rows, width_local)
    attn_new = ret[:, :, pos_dev].reshape(seqs, width_local)
    attention = jnp.concatenate([attn_rows, attn_new], 0)

    part = jnp.dot(attention, w_out, preferred_element_type=jnp.float32)
    summed = lax.psum_scatter(
        part.astype(jnp.bfloat16), "tp", scatter_dimension=1, tiled=True
    ).astype(jnp.float32)
    square = lax.psum(jnp.sum(summed * summed, -1), "tp")
    out = (
        local_rows.astype(jnp.float32)
        + summed * lax.rsqrt(square[:, None] / full_width + norm_eps) * post_gain
    ).astype(jnp.bfloat16)
    return (
        out[:prompt_rows].reshape(seqs, pos_dev, width_local),
        out[prompt_rows:],
    )


def solution(mesh):
    in_specs = (
        P(None, "seq", "tp"),
        P(None, "tp"),
        P(None, None, "tp"),
        P("tp", None),
        P("tp"),
        P("tp"),
        P("tp"),
        P(),
    )
    out_specs = (P(None, "seq", "tp"), P(None, "tp"))
    return jax.shard_map(body, mesh=mesh, in_specs=in_specs, out_specs=out_specs, check_vma=False)
```

time: 496 us -> 335 us (0.68)
  blocking collectives: 146 us -> 55.4 us
  waiting for transfers between devices: 254 us -> 197 us
  matrix products: 51.9 us -> 24.8 us
  starting transfers between devices: 0.16 us -> 7.54 us
    psum x1 -> x0, waiting for transfers between devices: 142 us -> none  [body(): lax.psum(part_rows.astype(jnp.bfloat16), 'tp').astype(jnp.float32)]
    all_gather x4 -> x0, blocking collectives: 92.8 us -> none  [the longest x3 64.2 us: joined(): everything = jax.tree.map(lambda part: lax.all_gather(part, axis), value)]
    reduce_scatter x0 -> x1, waiting for transfers between devices: none -> 88.1 us  [body(): lax.psum_scatter(part.astype(jnp.bfloat16), 'tp', scatter_dimension=1, ti...]
    dot_general x8 -> x6, matrix products: 51.9 us -> 24.8 us  [the longest x1 10.6 us: body(): jnp.einsum('tn,cnf->ctf', all_rows, w_qkv, preferred_element_type=jnp.flo...]
    all_to_all x0 -> x1, blocking collectives: none -> 19.6 us  [body(): ret = lax.all_to_all(back, 'seq', 0, 0, tiled=True)]
    all_gather x3 -> x1, waiting for transfers between devices: 110 us -> 92.7 us  [body(): all_rows = lax.all_gather(local_rows, 'tp', axis=1, tiled=True)]
    psum x2, blocking collectives: 53.1 us -> 35.8 us  [the longest x1 18.1 us: body(): lax.psum((jnp.sum(query_raw * query_raw, -1), jnp.sum(key_raw * key_raw,...]
    all_to_all x0 -> x1, waiting for transfers between devices: none -> 15.8 us  [body(): got = lax.all_to_all(qkv, 'seq', 0, 0, tiled=True)]
  transfers between devices with their start and end apart: 4 -> 3, of which waited for: 3 -> 3; matrix products, arithmetic and copies ran while one was open for 9% -> 2% of each run, Pallas kernels for 0% -> 0%
where the time goes in v1:
time: 335 us; the launch traced here: 334 us
  waiting for transfers between devices  197 us (59%)
  blocking collectives  55.4 us (17%)
  other arithmetic  27.2 us (8%)
  matrix products  24.8 us (7%)
  between operations  16.4 us (5%)
  starting transfers between devices  7.54 us (2%)
  local copies, waits for them, and re-layouts  6.41 us (2%)
    all_gather x1, waiting for transfers between devices, body(): all_rows = lax.all_gather(local_rows, 'tp', axis=1, tiled=True)  92.7 us
    reduce_scatter x1, waiting for transfers between devices, body(): lax.psum_scatter(part.astype(jnp.bfloat16), 'tp', scatter_dimension=1, ti...  88.1 us
    all_to_all x1, blocking collectives, body(): ret = lax.all_to_all(back, 'seq', 0, 0, tiled=True)  19.6 us
    psum x1, blocking collectives, body(): lax.psum((jnp.sum(query_raw * query_raw, -1), jnp.sum(key_raw * key_raw,...  18.1 us
    psum x1, blocking collectives, body(): square = lax.psum(jnp.sum(summed * summed, -1), 'tp')  17.7 us
    all_to_all x1, waiting for transfers between devices, body(): got = lax.all_to_all(qkv, 'seq', 0, 0, tiled=True)  15.8 us
    dot_general x1, matrix products, body(): jnp.einsum('tn,cnf->ctf', all_rows, w_qkv, preferred_element_type=jnp.flo...  10.6 us
    reduce_sum x1, other arithmetic, attend_pair(): total = jnp.sum(weights, -1, keepdims=True)  8.42 us
  transfers between devices with their start and end apart: 3, of which 3 were waited for; matrix products, arithmetic and copies ran while one was open for 2% of the time, Pallas kernels for 0%

profile of v1, /device:TPU:32, one launch (start us, length us, event | category | flops | bytes accessed | tf_op | source)
XLA Modules:
  0.0 334.3 jit_solution(7153203666881482094)
XLA Ops:
  7.2 0.0 copy-start.9
  7.2 0.0 all-gather.2.cloned.1.call-start
  7.2 1.9 pad_maximum_fusion.2
  9.1 0.0 all-gather.2.cloned.1.call-update
  9.2 0.0 copy-done.9
  9.2 1.7 multiply_cosine_fusion
  11.0 92.7 %all-gather.2.cloned.1.call-done = bf16[516,4096]{1,0:T(8,128)(2,1)} async-done(((bf16[516,512]{1,0:T(8,128)(2,1)}), bf16[516,4096]{1,0:T(8,128)(2,1)}) %all-gather.2.cloned.1.call-update) | async-done | bytes 4227088 | tf_op jit(solution)/shard_map/all_gather | solution.py:64
  103.6 10.6 %fusion.45 = (bf16[3,516,512]{2,1,0:T(8,128)(2,1)S(1)}, f32[3,516,512]{2,1,0:T(8,128)S(1)}) fusion(bf16[3,4096,512]{2,1,0:T(8,128)(2,1)} %param.10, bf16[516,4096]{1,0:T(8,128)(2,1)} %all-gather.2.cloned.1.call-done), kind=kOutput, calls=%fused_computation.82 | convolution fusion | flops 6493575168 | bytes 21565440 | tf_op jit(solution)/shard_map/tn,cnf->ctf/dot_general | solution.py:65
  114.3 0.0 copy-start.4
  114.3 0.3 multiply_reduce_fusion.1
  114.7 0.8 copy-done.4
  115.5 0.1 stack.14
  115.6 0.9 copy.12
  116.5 0.4 squeeze.27
  116.9 0.0 copy-start.6
  116.9 0.4 squeeze.28
  117.3 0.0 copy-start.7
  117.3 18.1 %all-reduce = (f32[516]{0:T(1024)S(1)}, f32[516]{0:T(1024)S(1)}) all-reduce(f32[516]{0:T(1024)S(1)} %get-tuple-element.3, f32[516]{0:T(1024)S(1)} %get-tuple-element.2), channel_id=1, replica_groups=mesh['seq'=16,'tp'=8] {'tp'}, use_global_device_ids=true, to_apply=%region_3.0 | all-reduce | flops 1032 | bytes 8256 | tf_op jit(solution)/shard_map/psum | solution.py:67
  135.4 0.0 copy-done.6
  135.4 1.5 multiply_multiply_fusion.1
  137.0 0.0 copy-start.3
  137.0 1.5 multiply_multiply_fusion
  138.5 1.7 add_convert_fusion.1
  140.3 0.7 fusion.27
  141.0 0.1 copy.10
  141.1 0.0 copy-start.2
  141.1 0.7 fusion.26
  141.8 0.0 copy-done
  141.8 0.1 copy.11
  141.9 0.2 copy-done.2
  142.1 1.3 pad_maximum_fusion
  143.5 7.3 %all-to-all-start = ((bf16[16,3,128,128]{3,2,1,0:T(8,128)(2,1)}), bf16[16,3,128,128]{3,2,1,0:T(8,128)(2,1)S(1)}, u32[]{:S(2)}, u32[]{:S(2)}) async-start(bf16[16,3,128,128]{3,2,1,0:T(8,128)(2,1)} %bitcast.10), calls=%async_computation | async-start | bytes 3145728 | tf_op jit(solution)/shard_map/all_to_all | solution.py:89
  150.7 0.2 reduce-scatter.2.cloned.1.call-start
  151.0 0.6 dynamic_slice.12
  151.6 0.7 iota_compare_fusion.1
  152.2 0.7 slice.101
  152.9 0.8 pad_maximum_fusion.4
  153.7 0.1 pad_maximum_fusion.3
  153.8 0.6 fusion.34
  155.0 15.8 %all-to-all-done = bf16[16,3,128,128]{3,2,1,0:T(8,128)(2,1)S(1)} async-done(((bf16[16,3,128,128]{3,2,1,0:T(8,128)(2,1)}), bf16[16,3,128,128]{3,2,1,0:T(8,128)(2,1)S(1)}, u32[]{:S(2)}, u32[]{:S(2)}) %all-to-all-start) | async-done | bytes 1572896 | tf_op jit(solution)/shard_map/all_to_all | solution.py:89
  170.8 0.1 fusion.44
  170.9 0.2 fusion.38
  171.1 1.3 fusion.28
  173.1 1.3 fusion.29
  175.0 5.9 %fusion.1 = (f32[2048]{0:T(1024)S(1)}, f32[2048,2048]{0,1:T(8,128)S(1)}) fusion(pred[2048]{0:T(1024)(128)(4,1)S(1)} %iota_compare_fusion.1, bf16[2048,128]{1,0:T(8,128)(2,1)S(1)} %bitcast.92, bf16[2048,128]{1,0:T(8,128)(2,1)S(1)} %bitcast.88), kind=kOutput, calls=%fused_computation.4 | convolution fusion | flops 1094711296 | bytes 17836032 | tf_op jit(solution)/shard_map/dot_general | solution.py:28
  180.9 8.4 %fusion.6 = f32[2048]{0:T(1024)S(1)} fusion(f32[2048]{0:T(1024)S(1)} %get-tuple-element.23, f32[2048,2048]{0,1:T(8,128)S(1)} %get-tuple-element.24, pred[2048]{0:T(1024)(128)(4,1)S(1)} %iota_compare_fusion.1), kind=kLoop, calls=%fused_computation.10 | loop fusion | flops 29358080 | bytes 16795648 | tf_op jit(solution)/shard_map/reduce_sum | solution.py:35
  189.3 3.5 %fusion.10 = bf16[2048,128]{1,0:T(8,128)(2,1)S(1)} fusion(bf16[2048,128]{1,0:T(8,128)(2,1)S(1)} %bitcast.85, f32[2048]{0:T(1024)S(1)} %get-tuple-element.23, f32[2048,2048]{0,1:T(8,128)S(1)} %get-tuple-element.24, pred[2048]{0:T(1024)(128)(4,1)S(1)} %iota_compare_fusion.1, f32[2048]{0:T(1024)S(1)} %fusion.6), kind=kOutput, calls=%fused_computation.12 | convolution fusion | flops 1103626240 | bytes 17844224 | tf_op jit(solution)/shard_map/dot_general | solution.py:37
  192.9 0.2 fusion.18
  193.1 0.0 copy-start.10
  193.1 19.6 %all_to_all.10 = bf16[16,136,128]{2,1,0:T(8,128)(2,1)S(1)} all-to-all(bf16[16,136,128]{2,1,0:T(8,128)(2,1)S(1)} %pad_maximum_fusion.1), channel_id=1, replica_groups=mesh['seq'=16,'tp'=8] {'seq'}, dimensions={0} | all-to-all | bytes 1114112 | tf_op jit(solution)/shard_map/all_to_all | solution.py:105
  212.7 0.1 copy.13
  212.8 0.2 slice_bitcast_fusion
  213.0 0.2 copy.14
  213.2 0.1 copy.22
  213.3 0.0 copy-done.10
  213.3 4.4 %convolution_convert_fusion = bf16[516,4096]{1,0:T(8,128)(2,1)} fusion(bf16[512,4096]{1,0:T(8,128)(2,1)S(1)} %copy-done.10, bf16[4,512]{1,0:T(4,128)(2,1)S(1)} %bitcast.98, bf16[512,512]{1,0:T(8,128)(2,1)S(1)} %bitcast.91), kind=kOutput, calls=%fused_computation.7 | convolution fusion | flops 2167431168 | bytes 8949760 | tf_op jit(solution)/shard_map/dot_general | solution.py:111
  217.7 0.0 reduce-scatter.2.cloned.1.call-update
  217.7 88.1 %reduce-scatter.2.cloned.1.call-done = bf16[516,512]{1,0:T(8,128)(2,1)} async-done(((bf16[516,4096]{1,0:T(8,128)(2,1)}), bf16[516,512]{1,0:T(8,128)(2,1)}) %reduce-scatter.2.cloned.1.call-update) | async-done | bytes 528400 | tf_op jit(solution)/shard_map/reduce_scatter | solution.py:112
  305.8 1.2 fusion.19
  307.0 17.7 %psum.23 = f32[516]{0:T(1024)S(1)} all-reduce(f32[516]{0:T(1024)S(1)} %fusion.19), channel_id=1, replica_groups=mesh['seq'=16,'tp'=8] {'tp'}, use_global_device_ids=true, to_apply=%region_10.11 | all-reduce | flops 516 | bytes 4128 | tf_op jit(solution)/shard_map/psum | solution.py:115
  324.7 0.0 copy-done.1
  324.8 1.3 fusion.22
  326.1 0.6 slice.105
  326.7 0.8 slice.104
  (21 shorter events, 0.2 us)
Async XLA Ops:
  7.2 2.0 copy-start.9
  7.2 96.5 %all-gather.2.cloned.1.call-start = ((), (), s32[]{:S(2)}) async-start(), calls=%async_computation.3 | async-start | bytes 4792320 | tf_op jit(solution)/shard_map/all_gather | solution.py:64
  114.3 1.2 copy-start.4
  116.9 18.5 %copy-start.6 = (f32[512]{0:T(512)S(1)}, f32[512]{0:T(512)}, u32[]{:S(2)}) copy-start(f32[512]{0:T(512)} %param.12) | copy-start | bytes 6148
  117.3 19.7 %copy-start.7 = (f32[512]{0:T(512)S(1)}, f32[512]{0:T(512)}, u32[]{:S(2)}) copy-start(f32[512]{0:T(512)} %param.13) | copy-start | bytes 6148
  137.0 1.6 copy-start.3
  140.3 1.6 copy-start
  141.1 1.0 copy-start.2
  143.5 27.3 %all-to-all-start = ((bf16[16,3,128,128]{3,2,1,0:T(8,128)(2,1)}), bf16[16,3,128,128]{3,2,1,0:T(8,128)(2,1)S(1)}, u32[]{:S(2)}, u32[]{:S(2)}) async-start(bf16[16,3,128,128]{3,2,1,0:T(8,128)(2,1)} %bitcast.10), calls=%async_computation | async-start | bytes 3145728 | tf_op jit(solution)/shard_map/all_to_all | solution.py:89
  150.7 155.0 %reduce-scatter.2.cloned.1.call-start = ((), (), s32[]{:S(2)}) async-start(), calls=%async_computation.4 | async-start | bytes 4792320 | tf_op jit(solution)/shard_map/reduce_scatter | solution.py:112
  193.1 20.2 %copy-start.10 = (bf16[512,4096]{1,0:T(8,128)(2,1)S(1)}, bf16[512,4096]{1,0:T(8,128)(2,1)}, u32[]{:S(2)}) copy-start(bf16[512,4096]{1,0:T(8,128)(2,1)} %param.11) | copy-start | bytes 12582916
  217.6 107.1 %copy-start.1 = (bf16[4,128,512]{2,1,0:T(8,128)(2,1)S(1)}, bf16[4,128,512]{2,1,0:T(8,128)(2,1)}, u32[]{:S(2)}) copy-start(bf16[4,128,512]{2,1,0:T(8,128)(2,1)} %param.8) | copy-start | bytes 1572868
  217.6 107.1 %copy-start.5 = (bf16[4,512]{1,0:T(4,128)(2,1)S(1)}, bf16[4,512]{1,0:T(4,128)(2,1)}, u32[]{:S(2)}) copy-start(bf16[4,512]{1,0:T(4,128)(2,1)} %param.9) | copy-start | bytes 12292
  217.7 107.1 %copy-start.8 = (f32[512]{0:T(512)S(1)}, f32[512]{0:T(512)}, u32[]{:S(2)}) copy-start(f32[512]{0:T(512)} %param.14) | copy-start | bytes 6148
Sparse Core Ops, SparseCore 0:
  9.7 93.9 all-gather.1
  217.8 87.9 reduce-scatter.1

commit v2 on v1

--- a/solution.py
+++ b/solution.py
@@ -20,6 +20,79 @@
     lower = values[..., :half]
     upper = values[..., half:]
     return jnp.concatenate([lower * cosine - upper * sine, upper * cosine + lower * sine], -1)
+
+
+def tp_links(width):
+    size = 8
+    cross = [(i, i ^ 1) for i in range(size)]
+    up = [(i, (i + 2) % size) for i in range(size)]
+    down = [(i, (i - 2) % size) for i in range(size)]
+    t = lax.axis_index("tp")
+    y, x = t // 2, t % 2
+    other = 1 - x
+
+    def block(dy, side):
+        return ((y + dy) % 4) * 2 + side
+
+    order = {
+        "own": block(0, x), "ax": block(0, other), "aup": block(-1, x), "adn": block(1, x),
+        "m1": block(1, other), "m2": block(-1, other), "m3": block(2, x), "m4": block(2, other),
+    }
+    return cross, up, down, order
+
+
+def tp_gather(piece):
+    width = piece.shape[1]
+    half, quarter = width // 2, width // 4
+    cross, up, down, order = tp_links(width)
+    send = lambda value, perm: lax.ppermute(value, "tp", perm)
+    ax = send(piece, cross)
+    aup = send(piece, up)
+    adn = send(piece, down)
+    bx = send(jnp.concatenate([adn[:, :half], aup[:, :half]], 1), cross)
+    bdn = send(jnp.concatenate([ax[:, half:], adn[:, :half]], 1), down)
+    bup = send(jnp.concatenate([ax[:, half:], aup[:, half:]], 1), up)
+    m1 = jnp.concatenate([bx[:, :half], bdn[:, :half]], 1)
+    m2 = jnp.concatenate([bx[:, half:], bup[:, :half]], 1)
+    m3 = jnp.concatenate([bdn[:, half:], bup[:, half:]], 1)
+    cx = send(m3[:, :half], cross)
+    cdn = send(m1[:, half:half + quarter], down)
+    cup = send(m2[:, half + quarter:], up)
+    m4 = jnp.concatenate([cx, cdn, cup], 1)
+    blocks = {"own": piece, "ax": ax, "aup": aup, "adn": adn, "m1": m1, "m2": m2, "m3": m3, "m4": m4}
+    whole = jnp.zeros((piece.shape[0], width * 8), piece.dtype)
+    for name, value in blocks.items():
+        whole = lax.dynamic_update_slice_in_dim(whole, value, order[name] * width, 1)
+    return whole
+
+
+def tp_reduce_scatter(part, width):
+    half, quarter = width // 2, width // 4
+    cross, up, down, order = tp_links(width)
+    send = lambda value, perm: lax.ppermute(value.astype(jnp.bfloat16), "tp", perm).astype(jnp.float32)
+    b = {name: lax.dynamic_slice_in_dim(part, index * width, width, 1) for name, index in order.items()}
+    rx = send(b["m4"][:, :half], cross)
+    rup = send(b["m4"][:, half:half + quarter], up)
+    rdn = send(b["m4"][:, half + quarter:], down)
+    m1, m2, m3 = b["m1"], b["m2"], b["m3"]
+    m3 = jnp.concatenate([m3[:, :half] + rx, m3[:, half:]], 1)
+    m1 = jnp.concatenate([m1[:, :half], m1[:, half:half + quarter] + rup, m1[:, half + quarter:]], 1)
+    m2 = jnp.concatenate([m2[:, :half + quarter], m2[:, half + quarter:] + rdn], 1)
+    rx = send(jnp.concatenate([m1[:, :half], m2[:, :half]], 1), cross)
+    rup = send(jnp.concatenate([m1[:, half:], m3[:, :half]], 1), up)
+    rdn = send(jnp.concatenate([m2[:, half:], m3[:, half:]], 1), down)
+    ax = jnp.concatenate([b["ax"][:, :half], b["ax"][:, half:] + rup[:, :half] + rdn[:, :half]], 1)
+    adn = jnp.concatenate([b["adn"][:, :half] + rx[:, :half] + rup[:, half:], b["adn"][:, half:]], 1)
+    aup = jnp.concatenate([b["aup"][:, :half] + rx[:, half:], b["aup"][:, half:] + rdn[:, half:]], 1)
+    return b["own"] + send(ax, cross) + send(adn, up) + send(aup, down)
+
+
+def tp_sum(values):
+    for bit in (1, 2, 4):
+        values = jax.tree.map(
+            lambda v, bit=bit: v + lax.ppermute(v, "tp", [(i, i ^ bit) for i in range(8)]), values
+        )
+    return values
 
 
 def attend_pair(q_all, k_all, v_all, q_new, k_new, v_new, length):
@@ -61,12 +134,10 @@
     full_len = pos_dev * n_seq
     flat_rows = tokens.reshape(prompt_rows, width_local)
     local_rows = jnp.concatenate([flat_rows, new_tokens], 0)
-    all_rows = lax.all_gather(local_rows, "tp", axis=1, tiled=True)
+    all_rows = tp_gather(local_rows)
     proj = jnp.einsum("tn,cnf->ctf", all_rows, w_qkv, preferred_element_type=jnp.float32)
     query_raw, key_raw = proj[0], proj[1]
-    query_sq, key_sq = lax.psum(
-        (jnp.sum(query_raw * query_raw, -1), jnp.sum(key_raw * key_raw, -1)), "tp"
-    )
+    query_sq, key_sq = tp_sum((jnp.sum(query_raw * query_raw, -1), jnp.sum(key_raw * key_raw, -1)))
 
     def normed(values, square_sum, gain):
         return values * lax.rsqrt(square_sum[:, None] / full_width + norm_eps) * gain
@@ -109,10 +180,8 @@
     attention = jnp.concatenate([attn_rows, attn_new], 0)
 
     part = jnp.dot(attention, w_out, preferred_element_type=jnp.float32)
-    summed = lax.psum_scatter(
-        part.astype(jnp.bfloat16), "tp", scatter_dimension=1, tiled=True
-    ).astype(jnp.float32)
-    square = lax.psum(jnp.sum(summed * summed, -1), "tp")
+    summed = tp_reduce_scatter(part, width_local)
+    square = tp_sum(jnp.sum(summed * summed, -1))
     out = (
         local_rows.astype(jnp.float32)
         + summed * lax.rsqrt(square[:, None] / full_width + norm_eps) * post_gain

time: 335 us -> 214 us (0.64)
  waiting for transfers between devices: 197 us -> 91.4 us
  blocking collectives: 55.4 us -> 0 us
  starting transfers between devices: 7.54 us -> 48.9 us
  between operations: 16.4 us -> 3.28 us
  other arithmetic: 27.2 us -> 34.9 us
  local copies, waits for them, and re-layouts: 6.41 us -> 13.7 us
  matrix products: 24.8 us -> 21.1 us
    all_gather x1 -> x0, waiting for transfers between devices: 92.7 us -> none  [body(): all_rows = lax.all_gather(local_rows, 'tp', axis=1, tiled=True)]
    reduce_scatter x1 -> x0, waiting for transfers between devices: 88.1 us -> none  [body(): lax.psum_scatter(part.astype(jnp.bfloat16), 'tp', scatter_dimension=1, ti...]
    ppermute x0 -> x27, waiting for transfers between devices: none -> 66.2 us  [the longest x9 27.5 us: tp_reduce_scatter(): lax.ppermute(value.astype(jnp.bfloat16), 'tp', perm).astype(jnp.float32)]
    psum x2 -> x0, blocking collectives: 35.8 us -> none  [the longest x1 18.1 us: body(): lax.psum((jnp.sum(query_raw * query_raw, -1), jnp.sum(key_raw * key_raw,...]
    ppermute x0 -> x27, starting transfers between devices: none -> 33.2 us  [the longest x9 12.1 us: tp_gather(): send = lambda value, perm: lax.ppermute(value, 'tp', perm)]
    all_to_all x1 -> x0, blocking collectives: 19.6 us -> none  [body(): ret = lax.all_to_all(back, 'seq', 0, 0, tiled=True)]
    all_to_all x0 -> x1, waiting for transfers between devices: none -> 9.07 us  [body(): ret = lax.all_to_all(back, 'seq', 0, 0, tiled=True)]
    all_to_all x0 -> x1, starting transfers between devices: none -> 8.04 us  [body(): ret = lax.all_to_all(back, 'seq', 0, 0, tiled=True)]
  transfers between devices with their start and end apart: 3 -> 29, of which waited for: 3 -> 19; matrix products, arithmetic and copies ran while one was open for 2% -> 7% of each run, Pallas kernels for 0% -> 0%
where the time goes in v2:
time: 214 us; the launch traced here: 213 us
  waiting for transfers between devices  91.4 us (43%)
  starting transfers between devices  48.9 us (23%)
  other arithmetic  34.9 us (16%)
  matrix products  21.1 us (10%)
  local copies, waits for them, and re-layouts  13.7 us (6%)
  between operations  3.28 us (2%)
    ppermute x9, waiting for transfers between devices, tp_reduce_scatter(): lax.ppermute(value.astype(jnp.bfloat16), 'tp', perm).astype(jnp.float32)  27.5 us
    ppermute x9, waiting for transfers between devices, tp_gather(): send = lambda value, perm: lax.ppermute(value, 'tp', perm)  25 us
    all_to_all x1, waiting for transfers between devices, body(): got = lax.all_to_all(qkv, 'seq', 0, 0, tiled=True)  16.1 us
    ppermute x9, waiting for transfers between devices, tp_sum(): lax.ppermute(v, 'tp', [(i, i ^ bit) for i in range(8)])  13.7 us
    ppermute x9, starting transfers between devices, tp_gather(): send = lambda value, perm: lax.ppermute(value, 'tp', perm)  12.1 us
    ppermute x9, starting transfers between devices, tp_reduce_scatter(): lax.ppermute(value.astype(jnp.bfloat16), 'tp', perm).astype(jnp.float32)  11.5 us
    ppermute x9, starting transfers between devices, tp_sum(): lax.ppermute(v, 'tp', [(i, i ^ bit) for i in range(8)])  9.58 us
    all_to_all x1, waiting for transfers between devices, body(): ret = lax.all_to_all(back, 'seq', 0, 0, tiled=True)  9.07 us
  transfers between devices with their start and end apart: 29, of which 19 were waited for; matrix products, arithmetic and copies ran while one was open for 7% of the time, Pallas kernels for 0%

profile of v2, /device:TPU:32, one launch (start us, length us, event | category | flops | bytes accessed | tf_op | source)
XLA Modules:
  0.0 213.3 jit_solution(1221829903436201670)
XLA Ops:
  0.7 2.5 %broadcast_in_dim.17 = bf16[516,4096]{1,0:T(8,128)(2,1)} broadcast(bf16[]{:T(256)} %constant.113.clone.1), dimensions={} | broadcast | bytes 4227074 | tf_op jit(solution)/shard_map/broadcast_in_dim | solution.py:63
  3.2 0.9 pad_maximum_fusion.5
  4.1 1.5 collective-permute-start
  5.6 1.6 collective-permute-start.1
  7.2 1.7 collective-permute-start.2
  8.8 9.1 %collective-permute-done = bf16[516,512]{1,0:T(8,128)(2,1)S(1)} collective-permute-done((bf16[516,512]{1,0:T(8,128)(2,1)S(1)}, bf16[516,512]{1,0:T(8,128)(2,1)S(1)}, u32[]{:S(2)}, u32[]{:S(2)}) %collective-permute-start) | collective-permute-done | bytes 528416 | tf_op jit(solution)/shard_map/ppermute | solution.py:48
  18.0 2.5 %collective-permute-done.1 = bf16[516,512]{1,0:T(8,128)(2,1)S(1)} collective-permute-done((bf16[516,512]{1,0:T(8,128)(2,1)S(1)}, bf16[516,512]{1,0:T(8,128)(2,1)S(1)}, u32[]{:S(2)}, u32[]{:S(2)}) %collective-permute-start.1) | collective-permute-done | bytes 528416 | tf_op jit(solution)/shard_map/ppermute | solution.py:48
  20.7 3.0 %collective-permute-start.4 = (bf16[516,512]{1,0:T(8,128)(2,1)S(1)}, bf16[516,512]{1,0:T(8,128)(2,1)S(1)}, u32[]{:S(2)}, u32[]{:S(2)}) collective-permute-start(bf16[516,512]{1,0:T(8,128)(2,1)S(1)} %get-tuple-element.40), channel_id=1, source_target_pairs={{0,6},{1,7},{2,0},{3,1},{4,2},{5,3},{6,4},{7,5},{8,14},{9,15},{10,... | collective-permute-start | bytes 1585160 | tf_op jit(solution)/shard_map/ppermute | solution.py:48
  24.2 0.9 constant_dynamic-update-slice_fusion.2
  25.1 0.9 constant_dynamic-update-slice_fusion.1
  26.0 0.9 constant_dynamic-update-slice_fusion
  26.8 10.3 %collective-permute-done.5 = bf16[516,512]{1,0:T(8,128)(2,1)S(1)} collective-permute-done((bf16[516,512]{1,0:T(8,128)(2,1)S(1)}, bf16[516,512]{1,0:T(8,128)(2,1)S(1)}, u32[]{:S(2)}, u32[]{:S(2)}) %collective-permute-start.5) | collective-permute-done | bytes 528416 | tf_op jit(solution)/shard_map/ppermute | solution.py:48
  37.2 3.3 %collective-permute-start.7 = (bf16[516,128]{1,0:T(8,128)(2,1)S(1)}, bf16[516,128]{1,0:T(8,128)(2,1)S(1)}, u32[]{:S(2)}, u32[]{:S(2)}) collective-permute-start(bf16[516,128]{1,0:T(8,128)(2,1)S(1)} %slice.257), channel_id=1, source_target_pairs={{0,6},{1,7},{2,0},{3,1},{4,2},{5,3},{6,4},{7,5},{8,14},{9,15},{10,... | collective-permute-start | bytes 396296 | tf_op jit(solution)/shard_map/ppermute | solution.py:48
  41.2 0.9 maximum_dynamic-update-slice_fusion
  42.1 0.9 maximum_dynamic-update-slice_fusion.1
  43.0 0.9 maximum_dynamic-update-slice_fusion.2
  43.9 3.1 %collective-permute-done.6 = bf16[516,256]{1,0:T(8,128)(2,1)S(1)} collective-permute-done((bf16[516,256]{1,0:T(8,128)(2,1)S(1)}, bf16[516,256]{1,0:T(8,128)(2,1)S(1)}, u32[]{:S(2)}, u32[]{:S(2)}) %collective-permute-start.6) | collective-permute-done | bytes 264224 | tf_op jit(solution)/shard_map/ppermute | solution.py:48
  47.1 0.9 maximum_dynamic-update-slice_fusion.3
  48.0 9.0 %fusion.55 = (bf16[3,516,512]{2,1,0:T(8,128)(2,1)S(1)}, f32[3,516,512]{2,1,0:T(8,128)S(1)}) fusion(bf16[3,4096,512]{2,1,0:T(8,128)(2,1)S(1)} %copy-done.13, bf16[516,4096]{1,0:T(8,128)(2,1)} %maximum_dynamic-update-slice_fusion.3), kind=kOutput, calls=%fused_computation.124 | convolution fusion | flops 6493575168 | bytes 21565440 | tf_op jit(solution)/shard_map/tn,cnf->ctf/dot_general | solution.py:138
  57.9 1.6 collective-permute-start.12
  59.5 1.5 collective-permute-done.9
  61.6 1.6 collective-permute-start.13
  63.1 1.5 collective-permute-done.10
  64.6 1.7 multiply_cosine_fusion
  66.5 0.9 copy.12
  68.1 3.6 %collective-permute-start.14 = (f32[516]{0:T(1024)S(1)}, f32[516]{0:T(1024)S(1)}, u32[]{:S(2)}, u32[]{:S(2)}) collective-permute-start(f32[516]{0:T(1024)S(1)} %add.254), channel_id=1, source_target_pairs={{0,4},{1,5},{2,6},{3,7},{4,0},{5,1},{6,2},{7,3},{8,12},{9,13},{10,... | collective-permute-start | bytes 6200 | tf_op jit(solution)/shard_map/ppermute | solution.py:93
  71.8 1.5 multiply_multiply_fusion.1
  73.4 1.5 multiply_multiply_fusion
  74.9 1.7 add_convert_fusion.2
  76.7 1.4 fusion.29
  79.2 1.3 pad_maximum_fusion
  80.5 7.6 %all-to-all-start = ((bf16[16,3,128,128]{3,2,1,0:T(8,128)(2,1)}), bf16[16,3,128,128]{3,2,1,0:T(8,128)(2,1)S(1)}, u32[]{:S(2)}, u32[]{:S(2)}) async-start(bf16[16,3,128,128]{3,2,1,0:T(8,128)(2,1)} %bitcast.10), calls=%async_computation | async-start | bytes 3145728 | tf_op jit(solution)/shard_map/all_to_all | solution.py:160
  92.1 16.1 %all-to-all-done = bf16[16,3,128,128]{3,2,1,0:T(8,128)(2,1)S(1)} async-done(((bf16[16,3,128,128]{3,2,1,0:T(8,128)(2,1)}), bf16[16,3,128,128]{3,2,1,0:T(8,128)(2,1)S(1)}, u32[]{:S(2)}, u32[]{:S(2)}) %all-to-all-start) | async-done | bytes 1572896 | tf_op jit(solution)/shard_map/all_to_all | solution.py:160
  108.5 1.3 fusion.33
  110.4 1.3 fusion.34
  112.4 5.9 %fusion.1 = (f32[2048]{0:T(1024)S(1)}, f32[2048,2048]{0,1:T(8,128)S(1)}) fusion(pred[2048]{0:T(1024)(128)(4,1)S(1)} %iota_compare_fusion.1, bf16[2048,128]{1,0:T(8,128)(2,1)S(1)} %bitcast.92, bf16[2048,128]{1,0:T(8,128)(2,1)S(1)} %bitcast.87), kind=kOutput, calls=%fused_computation.4 | convolution fusion | flops 1094711296 | bytes 17836032 | tf_op jit(solution)/shard_map/dot_general | solution.py:101
  118.3 8.4 %fusion.6 = f32[2048]{0:T(1024)S(1)} fusion(f32[2048]{0:T(1024)S(1)} %get-tuple-element.48, f32[2048,2048]{0,1:T(8,128)S(1)} %get-tuple-element.49, pred[2048]{0:T(1024)(128)(4,1)S(1)} %iota_compare_fusion.1), kind=kLoop, calls=%fused_computation.9 | loop fusion | flops 29358080 | bytes 16795648 | tf_op jit(solution)/shard_map/reduce_sum | solution.py:108
  126.7 3.5 %fusion.10 = bf16[2048,128]{1,0:T(8,128)(2,1)S(1)} fusion(bf16[2048,128]{1,0:T(8,128)(2,1)S(1)} %bitcast.84, f32[2048]{0:T(1024)S(1)} %get-tuple-element.48, f32[2048,2048]{0,1:T(8,128)S(1)} %get-tuple-element.49, pred[2048]{0:T(1024)(128)(4,1)S(1)} %iota_compare_fusion.1, f32[2048]{0:T(1024)S(1)} %fusion.6), kind=kOutput, calls=%fused_computation.11 | convolution fusion | flops 1103626240 | bytes 17844224 | tf_op jit(solution)/shard_map/dot_general | solution.py:110
  130.4 0.8 pad_maximum_fusion.3
  131.2 8.0 %all-to-all-start.1 = ((bf16[16,136,128]{2,1,0:T(8,128)(2,1)}), bf16[16,136,128]{2,1,0:T(8,128)(2,1)S(1)}, u32[]{:S(2)}, u32[]{:S(2)}) async-start(bf16[16,136,128]{2,1,0:T(8,128)(2,1)} %pad_maximum_fusion.3), calls=%async_computation.1 | async-start | bytes 1114112 | tf_op jit(solution)/shard_map/all_to_all | solution.py:176
  139.3 9.1 %all-to-all-done.1 = bf16[16,136,128]{2,1,0:T(8,128)(2,1)S(1)} async-done(((bf16[16,136,128]{2,1,0:T(8,128)(2,1)}), bf16[16,136,128]{2,1,0:T(8,128)(2,1)S(1)}, u32[]{:S(2)}, u32[]{:S(2)}) %all-to-all-start.1) | async-done | bytes 557088 | tf_op jit(solution)/shard_map/all_to_all | solution.py:176
  148.9 1.6 copy-done.2
  150.5 2.4 %fusion.25 = f32[516,4096]{1,0:T(8,128)S(1)} fusion(bf16[512,4096]{1,0:T(8,128)(2,1)S(1)} %copy-done.2, bf16[4,512]{1,0:T(4,128)(2,1)S(1)} %bitcast.95, bf16[512,512]{1,0:T(8,128)(2,1)S(1)} %bitcast.82), kind=kOutput, calls=%fused_computation.58 | convolution fusion | flops 2165317632 | bytes 13176832 | tf_op jit(solution)/shard_map/dot_general | solution.py:182
  153.4 0.9 collective-permute-start.15
  154.3 2.4 %collective-permute-start.18 = (bf16[516,128]{1,0:T(8,128)(2,1)S(1)}, bf16[516,128]{1,0:T(8,128)(2,1)S(1)}, u32[]{:S(2)}, u32[]{:S(2)}) collective-permute-start(bf16[516,128]{1,0:T(8,128)(2,1)S(1)} %get-tuple-element.26), channel_id=1, source_target_pairs={{0,6},{1,7},{2,0},{3,1},{4,2},{5,3},{6,4},{7,5},{8,14},{9,15},{10,... | collective-permute-start | bytes 396296 | tf_op jit(solution)/shard_map/ppermute | solution.py:72
  156.8 2.4 %collective-permute-start.21 = (bf16[516,512]{1,0:T(8,128)(2,1)S(1)}, bf16[516,512]{1,0:T(8,128)(2,1)S(1)}, u32[]{:S(2)}, u32[]{:S(2)}) collective-permute-start(bf16[516,512]{1,0:T(8,128)(2,1)S(1)} %pad_maximum_fusion.9), channel_id=1, source_target_pairs={{0,1},{1,0},{2,3},{3,2},{4,5},{5,4},{6,7},{7,6},{8,9},{9,8},{10,11... | collective-permute-start | bytes 1585160 | tf_op jit(solution)/shard_map/ppermute | solution.py:72
  159.2 1.7 collective-permute-done.15
  161.2 0.9 fusion.23
  162.1 2.7 %collective-permute-start.19 = (bf16[516,512]{1,0:T(8,128)(2,1)}, bf16[516,512]{1,0:T(8,128)(2,1)S(1)}, u32[]{:S(2)}, u32[]{:S(2)}) collective-permute-start(bf16[516,512]{1,0:T(8,128)(2,1)} %fusion.23), channel_id=1, source_target_pairs={{0,6},{1,7},{2,0},{3,1},{4,2},{5,3},{6,4},{7,5},{8,14},{9,15},{10,... | collective-permute-start | bytes 1585160 | tf_op jit(solution)/shard_map/ppermute | solution.py:72
  164.8 1.1 collective-permute-done.16
  166.4 10.3 %collective-permute-done.21 = bf16[516,512]{1,0:T(8,128)(2,1)S(1)} collective-permute-done((bf16[516,512]{1,0:T(8,128)(2,1)S(1)}, bf16[516,512]{1,0:T(8,128)(2,1)S(1)}, u32[]{:S(2)}, u32[]{:S(2)}) %collective-permute-start.21) | collective-permute-done | bytes 528416 | tf_op jit(solution)/shard_map/ppermute | solution.py:72
  176.9 3.2 %collective-permute-done.17 = bf16[516,512]{1,0:T(8,128)(2,1)S(1)} collective-permute-done((bf16[516,512]{1,0:T(8,128)(2,1)S(1)}, bf16[516,512]{1,0:T(8,128)(2,1)S(1)}, u32[]{:S(2)}, u32[]{:S(2)}) %collective-permute-start.17) | collective-permute-done | bytes 528416 | tf_op jit(solution)/shard_map/ppermute | solution.py:72
  180.2 2.0 fusion.22
  182.6 1.9 collective-permute-start.22
  185.2 8.9 %collective-permute-done.23 = bf16[516,512]{1,0:T(8,128)(2,1)S(1)} collective-permute-done((bf16[516,512]{1,0:T(8,128)(2,1)S(1)}, bf16[516,512]{1,0:T(8,128)(2,1)S(1)}, u32[]{:S(2)}, u32[]{:S(2)}) %collective-permute-start.23) | collective-permute-done | bytes 528416 | tf_op jit(solution)/shard_map/ppermute | solution.py:72
  194.1 2.1 %collective-permute-done.22 = bf16[516,512]{1,0:T(8,128)(2,1)S(1)} collective-permute-done((bf16[516,512]{1,0:T(8,128)(2,1)S(1)}, bf16[516,512]{1,0:T(8,128)(2,1)S(1)}, u32[]{:S(2)}, u32[]{:S(2)}) %collective-permute-start.22) | collective-permute-done | bytes 528416 | tf_op jit(solution)/shard_map/ppermute | solution.py:72
  196.2 1.6 multiply_reduce_fusion
  197.8 0.9 collective-permute-start.24
  198.7 2.8 %collective-permute-done.24 = f32[516]{0:T(1024)S(1)} collective-permute-done((f32[516]{0:T(1024)S(1)}, f32[516]{0:T(1024)S(1)}, u32[]{:S(2)}, u32[]{:S(2)}) %collective-permute-start.24) | collective-permute-done | bytes 2096 | tf_op jit(solution)/shard_map/ppermute | solution.py:93
  201.5 3.6 %collective-permute-done.25 = f32[516]{0:T(1024)S(1)} collective-permute-done((f32[516]{0:T(1024)S(1)}, f32[516]{0:T(1024)S(1)}, u32[]{:S(2)}, u32[]{:S(2)}) %collective-permute-start.25) | collective-permute-done | bytes 2096 | tf_op jit(solution)/shard_map/ppermute | solution.py:93
  205.1 1.3 collective-permute-start.26
  206.5 3.8 %collective-permute-done.26 = f32[516]{0:T(1024)S(1)} collective-permute-done((f32[516]{0:T(1024)S(1)}, f32[516]{0:T(1024)S(1)}, u32[]{:S(2)}, u32[]{:S(2)}) %collective-permute-start.26) | collective-permute-done | bytes 2096 | tf_op jit(solution)/shard_map/ppermute | solution.py:93
  210.3 1.6 add_convert_fusion
  211.9 0.8 slice.289
  (116 shorter events, 12.7 us)
Async XLA Ops:
  0.7 2.5 %copy-start.3 = (bf16[4,128,512]{2,1,0:T(8,128)(2,1)S(1)}, bf16[4,128,512]{2,1,0:T(8,128)(2,1)}, u32[]{:S(2)}) copy-start(bf16[4,128,512]{2,1,0:T(8,128)(2,1)} %param.8) | copy-start | bytes 1572868
  0.7 2.5 %copy-start.8 = (bf16[4,512]{1,0:T(4,128)(2,1)S(1)}, bf16[4,512]{1,0:T(4,128)(2,1)}, u32[]{:S(2)}) copy-start(bf16[4,512]{1,0:T(4,128)(2,1)} %param.9) | copy-start | bytes 12292
  4.1 13.8 %collective-permute-start = (bf16[516,512]{1,0:T(8,128)(2,1)S(1)}, bf16[516,512]{1,0:T(8,128)(2,1)S(1)}, u32[]{:S(2)}, u32[]{:S(2)}) collective-permute-start(bf16[516,512]{1,0:T(8,128)(2,1)S(1)} %get-tuple-element.37), channel_id=1, source_target_pairs={{0,1},{1,0},{2,3},{3,2},{4,5},{5,4},{6,7},{7,6},{8,9},{9,8},{10,11... | collective-permute-start | bytes 1585160 | tf_op jit(solution)/shard_map/ppermute | solution.py:48
  5.6 14.9 %collective-permute-start.1 = (bf16[516,512]{1,0:T(8,128)(2,1)S(1)}, bf16[516,512]{1,0:T(8,128)(2,1)S(1)}, u32[]{:S(2)}, u32[]{:S(2)}) collective-permute-start(bf16[516,512]{1,0:T(8,128)(2,1)S(1)} %get-tuple-element.37), channel_id=1, source_target_pairs={{0,2},{1,3},{2,4},{3,5},{4,6},{5,7},{6,0},{7,1},{8,10},{9,11},{10,... | collective-permute-start | bytes 1585160 | tf_op jit(solution)/shard_map/ppermute | solution.py:48
  7.2 13.4 %collective-permute-start.2 = (bf16[516,512]{1,0:T(8,128)(2,1)S(1)}, bf16[516,512]{1,0:T(8,128)(2,1)S(1)}, u32[]{:S(2)}, u32[]{:S(2)}) collective-permute-start(bf16[516,512]{1,0:T(8,128)(2,1)S(1)} %get-tuple-element.37), channel_id=1, source_target_pairs={{0,6},{1,7},{2,0},{3,1},{4,2},{5,3},{6,4},{7,5},{8,14},{9,15},{10,... | collective-permute-start | bytes 1585160 | tf_op jit(solution)/shard_map/ppermute | solution.py:48
  20.6 27.4 %copy-start.13 = (bf16[3,4096,512]{2,1,0:T(8,128)(2,1)S(1)}, bf16[3,4096,512]{2,1,0:T(8,128)(2,1)}, u32[]{:S(2)}) copy-start(bf16[3,4096,512]{2,1,0:T(8,128)(2,1)} %param.10) | copy-start | bytes 37748740
  20.7 16.5 %collective-permute-start.4 = (bf16[516,512]{1,0:T(8,128)(2,1)S(1)}, bf16[516,512]{1,0:T(8,128)(2,1)S(1)}, u32[]{:S(2)}, u32[]{:S(2)}) collective-permute-start(bf16[516,512]{1,0:T(8,128)(2,1)S(1)} %get-tuple-element.40), channel_id=1, source_target_pairs={{0,6},{1,7},{2,0},{3,1},{4,2},{5,3},{6,4},{7,5},{8,14},{9,15},{10,... | collective-permute-start | bytes 1585160 | tf_op jit(solution)/shard_map/ppermute | solution.py:48
  23.7 13.4 %collective-permute-start.5 = (bf16[516,512]{1,0:T(8,128)(2,1)S(1)}, bf16[516,512]{1,0:T(8,128)(2,1)S(1)}, u32[]{:S(2)}, u32[]{:S(2)}) collective-permute-start(bf16[516,512]{1,0:T(8,128)(2,1)S(1)} %get-tuple-element.39), channel_id=1, source_target_pairs={{0,2},{1,3},{2,4},{3,5},{4,6},{5,7},{6,0},{7,1},{8,10},{9,11},{10,... | collective-permute-start | bytes 1585160 | tf_op jit(solution)/shard_map/ppermute | solution.py:48
  23.7 17.5 %collective-permute-start.3 = (bf16[516,512]{1,0:T(8,128)(2,1)S(1)}, bf16[516,512]{1,0:T(8,128)(2,1)S(1)}, u32[]{:S(2)}, u32[]{:S(2)}) collective-permute-start(bf16[516,512]{1,0:T(8,128)(2,1)S(1)} %get-tuple-element.41), channel_id=1, source_target_pairs={{0,1},{1,0},{2,3},{3,2},{4,5},{5,4},{6,7},{7,6},{8,9},{9,8},{10,11... | collective-permute-start | bytes 1585160 | tf_op jit(solution)/shard_map/ppermute | solution.py:48
  37.1 6.8 %collective-permute-start.8 = (bf16[516,128]{1,0:T(8,128)(2,1)S(1)}, bf16[516,128]{1,0:T(8,128)(2,1)S(1)}, u32[]{:S(2)}, u32[]{:S(2)}) collective-permute-start(bf16[516,128]{1,0:T(8,128)(2,1)S(1)} %slice.258), channel_id=1, source_target_pairs={{0,2},{1,3},{2,4},{3,5},{4,6},{5,7},{6,0},{7,1},{8,10},{9,11},{10,... | collective-permute-start | bytes 396296 | tf_op jit(solution)/shard_map/ppermute | solution.py:48
  37.2 6.7 %collective-permute-start.7 = (bf16[516,128]{1,0:T(8,128)(2,1)S(1)}, bf16[516,128]{1,0:T(8,128)(2,1)S(1)}, u32[]{:S(2)}, u32[]{:S(2)}) collective-permute-start(bf16[516,128]{1,0:T(8,128)(2,1)S(1)} %slice.257), channel_id=1, source_target_pairs={{0,6},{1,7},{2,0},{3,1},{4,2},{5,3},{6,4},{7,5},{8,14},{9,15},{10,... | collective-permute-start | bytes 396296 | tf_op jit(solution)/shard_map/ppermute | solution.py:48
  40.6 6.5 %collective-permute-start.6 = (bf16[516,256]{1,0:T(8,128)(2,1)S(1)}, bf16[516,256]{1,0:T(8,128)(2,1)S(1)}, u32[]{:S(2)}, u32[]{:S(2)}) collective-permute-start(bf16[516,256]{1,0:T(8,128)(2,1)S(1)} %get-tuple-element.29), channel_id=1, source_target_pairs={{0,1},{1,0},{2,3},{3,2},{4,5},{5,4},{6,7},{7,6},{8,9},{9,8},{10,11... | collective-permute-start | bytes 792584 | tf_op jit(solution)/shard_map/ppermute | solution.py:48
  56.9 9.4 %copy-start.7 = (bf16[3,516,512]{2,1,0:T(8,128)(2,1)}, bf16[3,516,512]{2,1,0:T(8,128)(2,1)S(1)}, u32[]{:S(2)}) copy-start(bf16[3,516,512]{2,1,0:T(8,128)(2,1)S(1)} %get-tuple-element.46) | copy-start | bytes 4755460
  56.9 0.9 copy-start.12
  57.3 3.7 %collective-permute-start.9 = (f32[516]{0:T(1024)S(1)}, f32[516]{0:T(1024)S(1)}, u32[]{:S(2)}, u32[]{:S(2)}) collective-permute-start(f32[516]{0:T(1024)S(1)} %get-tuple-element.2), channel_id=1, source_target_pairs={{0,1},{1,0},{2,3},{3,2},{4,5},{5,4},{6,7},{7,6},{8,9},{9,8},{10,11... | collective-permute-start | bytes 6200 | tf_op jit(solution)/shard_map/ppermute | solution.py:93
  57.9 3.7 %collective-permute-start.12 = (f32[516]{0:T(1024)S(1)}, f32[516]{0:T(1024)S(1)}, u32[]{:S(2)}, u32[]{:S(2)}) collective-permute-start(f32[516]{0:T(1024)S(1)} %get-tuple-element.3), channel_id=1, source_target_pairs={{0,1},{1,0},{2,3},{3,2},{4,5},{5,4},{6,7},{7,6},{8,9},{9,8},{10,11... | collective-permute-start | bytes 6200 | tf_op jit(solution)/shard_map/ppermute | solution.py:93
  61.0 3.6 %collective-permute-start.10 = (f32[516]{0:T(1024)S(1)}, f32[516]{0:T(1024)S(1)}, u32[]{:S(2)}, u32[]{:S(2)}) collective-permute-start(f32[516]{0:T(1024)S(1)} %add.246), channel_id=1, source_target_pairs={{0,2},{1,3},{2,0},{3,1},{4,6},{5,7},{6,4},{7,5},{8,10},{9,11},{10,... | collective-permute-start | bytes 6200 | tf_op jit(solution)/shard_map/ppermute | solution.py:93
  61.6 6.6 %collective-permute-start.13 = (f32[516]{0:T(1024)S(1)}, f32[516]{0:T(1024)S(1)}, u32[]{:S(2)}, u32[]{:S(2)}) collective-permute-start(f32[516]{0:T(1024)S(1)} %add.253), channel_id=1, source_target_pairs={{0,2},{1,3},{2,0},{3,1},{4,6},{5,7},{6,4},{7,5},{8,10},{9,11},{10,... | collective-permute-start | bytes 6200 | tf_op jit(solution)/shard_map/ppermute | solution.py:93
  64.6 7.1 %collective-permute-start.11 = (f32[516]{0:T(1024)S(1)}, f32[516]{0:T(1024)S(1)}, u32[]{:S(2)}, u32[]{:S(2)}) collective-permute-start(f32[516]{0:T(1024)S(1)} %add.247), channel_id=1, source_target_pairs={{0,4},{1,5},{2,6},{3,7},{4,0},{5,1},{6,2},{7,3},{8,12},{9,13},{10,... | collective-permute-start | bytes 6200 | tf_op jit(solution)/shard_map/ppermute | solution.py:93
  67.7 4.0 %copy-start.10 = (f32[512]{0:T(512)S(1)}, f32[512]{0:T(512)}, u32[]{:S(2)}) copy-start(f32[512]{0:T(512)} %param.12) | copy-start | bytes 6148
  68.1 5.2 %collective-permute-start.14 = (f32[516]{0:T(1024)S(1)}, f32[516]{0:T(1024)S(1)}, u32[]{:S(2)}, u32[]{:S(2)}) collective-permute-start(f32[516]{0:T(1024)S(1)} %add.254), channel_id=1, source_target_pairs={{0,4},{1,5},{2,6},{3,7},{4,0},{5,1},{6,2},{7,3},{8,12},{9,13},{10,... | collective-permute-start | bytes 6200 | tf_op jit(solution)/shard_map/ppermute | solution.py:93
  71.8 1.6 copy-start.11
  73.4 1.6 copy-start.6
  76.7 1.4 copy-start.1
  78.1 1.0 copy-start.5
  80.5 27.7 %all-to-all-start = ((bf16[16,3,128,128]{3,2,1,0:T(8,128)(2,1)}), bf16[16,3,128,128]{3,2,1,0:T(8,128)(2,1)S(1)}, u32[]{:S(2)}, u32[]{:S(2)}) async-start(bf16[16,3,128,128]{3,2,1,0:T(8,128)(2,1)} %bitcast.10), calls=%async_computation | async-start | bytes 3145728 | tf_op jit(solution)/shard_map/all_to_all | solution.py:160
  131.2 17.1 %all-to-all-start.1 = ((bf16[16,136,128]{2,1,0:T(8,128)(2,1)}), bf16[16,136,128]{2,1,0:T(8,128)(2,1)S(1)}, u32[]{:S(2)}, u32[]{:S(2)}) async-start(bf16[16,136,128]{2,1,0:T(8,128)(2,1)} %pad_maximum_fusion.3), calls=%async_computation.1 | async-start | bytes 1114112 | tf_op jit(solution)/shard_map/all_to_all | solution.py:176
  148.3 2.2 %copy-start.2 = (bf16[512,4096]{1,0:T(8,128)(2,1)S(1)}, bf16[512,4096]{1,0:T(8,128)(2,1)}, u32[]{:S(2)}) copy-start(bf16[512,4096]{1,0:T(8,128)(2,1)} %param.11) | copy-start | bytes 12582916
  153.0 13.0 %copy-start = (f32[516,4096]{1,0:T(8,128)}, f32[516,4096]{1,0:T(8,128)S(1)}, u32[]{:S(2)}) copy-start(f32[516,4096]{1,0:T(8,128)S(1)} %fusion.25) | copy-start | bytes 25362436
  153.4 7.5 %collective-permute-start.15 = (bf16[516,128]{1,0:T(8,128)(2,1)S(1)}, bf16[516,128]{1,0:T(8,128)(2,1)S(1)}, u32[]{:S(2)}, u32[]{:S(2)}) collective-permute-start(bf16[516,128]{1,0:T(8,128)(2,1)S(1)} %get-tuple-element.25), channel_id=1, source_target_pairs={{0,2},{1,3},{2,4},{3,5},{4,6},{5,7},{6,0},{7,1},{8,10},{9,11},{10,... | collective-permute-start | bytes 396296 | tf_op jit(solution)/shard_map/ppermute | solution.py:72
  154.3 6.8 %collective-permute-start.18 = (bf16[516,128]{1,0:T(8,128)(2,1)S(1)}, bf16[516,128]{1,0:T(8,128)(2,1)S(1)}, u32[]{:S(2)}, u32[]{:S(2)}) collective-permute-start(bf16[516,128]{1,0:T(8,128)(2,1)S(1)} %get-tuple-element.26), channel_id=1, source_target_pairs={{0,6},{1,7},{2,0},{3,1},{4,2},{5,3},{6,4},{7,5},{8,14},{9,15},{10,... | collective-permute-start | bytes 396296 | tf_op jit(solution)/shard_map/ppermute | solution.py:72
  156.7 9.2 %collective-permute-start.16 = (bf16[516,256]{1,0:T(8,128)(2,1)S(1)}, bf16[516,256]{1,0:T(8,128)(2,1)S(1)}, u32[]{:S(2)}, u32[]{:S(2)}) collective-permute-start(bf16[516,256]{1,0:T(8,128)(2,1)S(1)} %slice.278), channel_id=1, source_target_pairs={{0,1},{1,0},{2,3},{3,2},{4,5},{5,4},{6,7},{7,6},{8,9},{9,8},{10,11... | collective-permute-start | bytes 792584 | tf_op jit(solution)/shard_map/ppermute | solution.py:72
  156.8 19.9 %collective-permute-start.21 = (bf16[516,512]{1,0:T(8,128)(2,1)S(1)}, bf16[516,512]{1,0:T(8,128)(2,1)S(1)}, u32[]{:S(2)}, u32[]{:S(2)}) collective-permute-start(bf16[516,512]{1,0:T(8,128)(2,1)S(1)} %pad_maximum_fusion.9), channel_id=1, source_target_pairs={{0,1},{1,0},{2,3},{3,2},{4,5},{5,4},{6,7},{7,6},{8,9},{9,8},{10,11... | collective-permute-start | bytes 1585160 | tf_op jit(solution)/shard_map/ppermute | solution.py:72
  162.1 14.7 %collective-permute-start.19 = (bf16[516,512]{1,0:T(8,128)(2,1)}, bf16[516,512]{1,0:T(8,128)(2,1)S(1)}, u32[]{:S(2)}, u32[]{:S(2)}) collective-permute-start(bf16[516,512]{1,0:T(8,128)(2,1)} %fusion.23), channel_id=1, source_target_pairs={{0,6},{1,7},{2,0},{3,1},{4,2},{5,3},{6,4},{7,5},{8,14},{9,15},{10,... | collective-permute-start | bytes 1585160 | tf_op jit(solution)/shard_map/ppermute | solution.py:72
  166.1 14.0 %collective-permute-start.17 = (bf16[516,512]{1,0:T(8,128)(2,1)S(1)}, bf16[516,512]{1,0:T(8,128)(2,1)S(1)}, u32[]{:S(2)}, u32[]{:S(2)}) collective-permute-start(bf16[516,512]{1,0:T(8,128)(2,1)S(1)} %pad_maximum_fusion.7), channel_id=1, source_target_pairs={{0,2},{1,3},{2,4},{3,5},{4,6},{5,7},{6,0},{7,1},{8,10},{9,11},{10,... | collective-permute-start | bytes 1585160 | tf_op jit(solution)/shard_map/ppermute | solution.py:72
  182.2 11.8 %collective-permute-start.23 = (bf16[516,512]{1,0:T(8,128)(2,1)S(1)}, bf16[516,512]{1,0:T(8,128)(2,1)S(1)}, u32[]{:S(2)}, u32[]{:S(2)}) collective-permute-start(bf16[516,512]{1,0:T(8,128)(2,1)S(1)} %pad_maximum_fusion.11), channel_id=1, source_target_pairs={{0,6},{1,7},{2,0},{3,1},{4,2},{5,3},{6,4},{7,5},{8,14},{9,15},{10,... | collective-permute-start | bytes 1585160 | tf_op jit(solution)/shard_map/ppermute | solution.py:72
  182.6 13.6 %collective-permute-start.22 = (bf16[516,512]{1,0:T(8,128)(2,1)S(1)}, bf16[516,512]{1,0:T(8,128)(2,1)S(1)}, u32[]{:S(2)}, u32[]{:S(2)}) collective-permute-start(bf16[516,512]{1,0:T(8,128)(2,1)S(1)} %pad_maximum_fusion.10), channel_id=1, source_target_pairs={{0,2},{1,3},{2,4},{3,5},{4,6},{5,7},{6,0},{7,1},{8,10},{9,11},{10,... | collective-permute-start | bytes 1585160 | tf_op jit(solution)/shard_map/ppermute | solution.py:72
  184.5 25.8 %copy-start.4 = (bf16[4,128,512]{2,1,0:T(8,128)(2,1)S(1)}, bf16[4,128,512]{2,1,0:T(8,128)(2,1)}, u32[]{:S(2)}) copy-start(bf16[4,128,512]{2,1,0:T(8,128)(2,1)} %param.8) | copy-start | bytes 1572868
  184.5 25.8 %copy-start.9 = (f32[512]{0:T(512)S(1)}, f32[512]{0:T(512)}, u32[]{:S(2)}) copy-start(f32[512]{0:T(512)} %param.14) | copy-start | bytes 6148
  184.5 11.7 %collective-permute-start.20 = (bf16[516,512]{1,0:T(8,128)(2,1)S(1)}, bf16[516,512]{1,0:T(8,128)(2,1)S(1)}, u32[]{:S(2)}, u32[]{:S(2)}) collective-permute-start(bf16[516,512]{1,0:T(8,128)(2,1)S(1)} %pad_maximum_fusion.8), channel_id=1, source_target_pairs={{0,1},{1,0},{2,3},{3,2},{4,5},{5,4},{6,7},{7,6},{8,9},{9,8},{10,11... | collective-permute-start | bytes 1585160 | tf_op jit(solution)/shard_map/ppermute | solution.py:72
  197.8 3.7 %collective-permute-start.24 = (f32[516]{0:T(1024)S(1)}, f32[516]{0:T(1024)S(1)}, u32[]{:S(2)}, u32[]{:S(2)}) collective-permute-start(f32[516]{0:T(1024)S(1)} %multiply_reduce_fusion), channel_id=1, source_target_pairs={{0,1},{1,0},{2,3},{3,2},{4,5},{5,4},{6,7},{7,6},{8,9},{9,8},{10,11... | collective-permute-start | bytes 6200 | tf_op jit(solution)/shard_map/ppermute | solution.py:93
  201.5 3.6 %collective-permute-start.25 = (f32[516]{0:T(1024)S(1)}, f32[516]{0:T(1024)S(1)}, u32[]{:S(2)}, u32[]{:S(2)}) collective-permute-start(f32[516]{0:T(1024)S(1)} %add.273), channel_id=1, source_target_pairs={{0,2},{1,3},{2,0},{3,1},{4,6},{5,7},{6,4},{7,5},{8,10},{9,11},{10,... | collective-permute-start | bytes 6200 | tf_op jit(solution)/shard_map/ppermute | solution.py:93
  205.1 5.1 %collective-permute-start.26 = (f32[516]{0:T(1024)S(1)}, f32[516]{0:T(1024)S(1)}, u32[]{:S(2)}, u32[]{:S(2)}) collective-permute-start(f32[516]{0:T(1024)S(1)} %add.274), channel_id=1, source_target_pairs={{0,4},{1,5},{2,6},{3,7},{4,0},{5,1},{6,2},{7,3},{8,12},{9,13},{10,... | collective-permute-start | bytes 6200 | tf_op jit(solution)/shard_map/ppermute | solution.py:93
